TPU v7x, 128 devices: a whole 4x4x4 slice. The times are simulated.
128 devices in a mesh: fsdp: 8 (over x, z_lo), dp: 16 (over z_hi, y, core).
Axes of the slice: x: 4, y: 4, z: 4 (z_hi: 2, z_lo: 2; z = z_hi * 2 + z_lo), core: 2. Of those that a mesh axis runs over, the one named last changes fastest.
Arguments:
- tokens: bfloat16 [8, 2176, 3200], P('fsdp', 'dp'), may hold values from -6 to 6
- norm_gain: float32 [3200], replicated, may hold values from 0.5 to 1.5
- qkv_weight: bfloat16 [3200, 6144], P('fsdp', 'dp'), may hold values from -4 to 4
- qk_gain: float32 [2, 2048], P(None, 'dp'), may hold values from 1 to 8
- out_weight: bfloat16 [2048, 3200], P('dp', 'fsdp'), may hold values from -0.125 to 0.125
- layer_scale: float32 [3200], replicated, may hold values from 0.2 to 1
- tile_counts: int32 [8, 2], replicated, may hold values from 0 to 2, as said below
- owners: int32 [8, 2], replicated, may hold values from 0 to 7, as said below
Outputs:
- vision_tokens: bfloat16 [32, 256, 12800], P('fsdp', None, 'dp')
Inputs may be any that keep to these rules, and one draw needn't show every extreme that they name: `tile_counts`: column 0 is 1 to 2, column 1 is 0 to 2 minus column 0. All owners together get at most 4 live tiles each, and one owner gets exactly 4.
All inputs are finite; a program needn't handle non-finite values.
Results may differ from a plain program's by a relative error of at most 0.006.
The roundings to bfloat16 on the way count: a program that leaves them out, or rounds other values in their place, can miss the bound.
Values may be sent and summed in bfloat16 or wider, within the bound.
No kernel may reach another device: no remote copies, remote signals or barrier semaphores. Data moves between devices by JAX's collectives and lax.ppermute only.
A program may use at most 192 MiB of HBM per device.

v0:
```python
import jax
import jax.numpy as jnp
from jax import lax
from jax.sharding import PartitionSpec as P

HEAD_DIM = 128
GRID = 32
SLOTS = 2
TILE = 1025
CAP = 4
EPSILON = 1e-06


def merge_tiles(values):
    halves = GRID // 2
    columns = values.shape[1]
    tile_list = []
    for tile_slot in range(SLOTS):
        patches = values[tile_slot * TILE + 1 : (tile_slot + 1) * TILE]
        square = patches.reshape(halves, 2, halves, 2, columns).transpose(0, 2, 4, 1, 3)
        tile_list.append(square.reshape(halves * halves, columns * 4))
    return jnp.stack(tile_list)


def tile_owners(tile_counts, owners):
    slot_index = jnp.arange(SLOTS, dtype=jnp.int32)[None, :]
    first_count = tile_counts[:, 0:1]
    holder = jnp.where(slot_index < first_count, owners[:, 0:1], owners[:, 1:2])
    living = slot_index < first_count + tile_counts[:, 1:2]
    return (holder, living)


def place_tiles(received, holder, living, target):
    owned_flag = jnp.logical_and(living, holder == target).reshape(-1).astype(jnp.int32)
    before = jnp.cumsum(owned_flag) - owned_flag
    chosen = jnp.logical_and(
        before[None, :] == jnp.arange(CAP, dtype=jnp.int32)[:, None], owned_flag[None, :] == 1
    )
    flattened = received.reshape(received.shape[0] * received.shape[1], -1)
    placed = jnp.dot(chosen.astype(jnp.bfloat16), flattened, preferred_element_type=jnp.float32)
    return placed.astype(jnp.bfloat16).reshape(CAP, received.shape[2], received.shape[3])


def body(tokens, norm_gain, qkv_weight, qk_gain, out_weight, layer_scale, tile_counts, owners):
    own_rows = tokens[0]
    gathered = lax.all_gather(own_rows, "dp", axis=0, tiled=True)
    length = gathered.shape[0]
    model_width = gathered.shape[1]
    groups = lax.axis_size("dp")
    values = gathered.astype(jnp.float32)
    normed = (
        values * lax.rsqrt(jnp.mean(values * values, axis=-1, keepdims=True) + EPSILON) * norm_gain
    ).astype(jnp.bfloat16)
    projected = jnp.dot(
        normed,
        lax.all_gather(qkv_weight, "fsdp", axis=0, tiled=True),
        preferred_element_type=jnp.float32,
    )
    queries = projected[:, :HEAD_DIM]
    keys_part = projected[:, HEAD_DIM : 2 * HEAD_DIM]
    values_part = projected[:, 2 * HEAD_DIM :].astype(jnp.bfloat16)
    query_sums, key_sums = lax.psum(
        (jnp.sum(queries * queries, axis=-1), jnp.sum(keys_part * keys_part, axis=-1)), "dp"
    )
    window = groups * HEAD_DIM
    queries = (queries * lax.rsqrt(query_sums / window + EPSILON)[:, None] * qk_gain[0]).astype(
        jnp.bfloat16
    )
    keys_part = (keys_part * lax.rsqrt(key_sums / window + EPSILON)[:, None] * qk_gain[1]).astype(
        jnp.bfloat16
    )
    row_index = lax.axis_index("fsdp")
    row_count = lax.axis_size("fsdp")
    factor = HEAD_DIM ** (-0.5)
    covered = SLOTS * TILE
    tile_query = queries[:covered].reshape(SLOTS, TILE, HEAD_DIM)
    tile_key = keys_part[:covered].reshape(SLOTS, TILE, HEAD_DIM)
    tile_value = values_part[:covered].reshape(SLOTS, TILE, HEAD_DIM)
    scores = (
        jnp.einsum("sqc,skc->sqk", tile_query, tile_key, preferred_element_type=jnp.float32)
        * factor
    )
    highest = jnp.max(scores, axis=-1, keepdims=True)
    exponent = jnp.exp(scores - highest)
    weights = (exponent / jnp.sum(exponent, axis=-1, keepdims=True)).astype(jnp.bfloat16)
    tile_out = jnp.einsum(
        "sqk,skc->sqc", weights, tile_value, preferred_element_type=jnp.float32
    ).astype(jnp.bfloat16)
    head_out = jnp.concatenate(
        [
            tile_out.reshape(covered, HEAD_DIM),
            jnp.zeros((length - covered, HEAD_DIM), jnp.bfloat16),
        ],
        axis=0,
    )
    dp_index = lax.axis_index("dp")
    block = model_width // groups
    head_rows = lax.all_gather(out_weight, "fsdp", axis=1, tiled=True)
    weight_block = lax.all_to_all(head_rows, "dp", split_axis=1, concat_axis=0, tiled=True)
    all_heads = lax.all_gather(head_out, "dp", axis=0, tiled=False)
    head_terms = jnp.einsum(
        "hsc,hcd->hsd",
        all_heads,
        weight_block.reshape(groups, HEAD_DIM, block),
        preferred_element_type=jnp.float32,
    ).astype(jnp.bfloat16)
    attention = jnp.sum(lax.optimization_barrier(head_terms).astype(jnp.float32), axis=0)
    own_block = lax.dynamic_slice_in_dim(gathered, dp_index * block, block, axis=1)
    scale_block = lax.dynamic_slice_in_dim(layer_scale, dp_index * block, block)
    updated = (own_block.astype(jnp.float32) + scale_block * attention).astype(jnp.bfloat16)
    merged = merge_tiles(updated)
    holder, living = tile_owners(tile_counts, owners)
    own_holder = holder[row_index]
    own_living = living[row_index]
    destination = jnp.arange(row_count, dtype=jnp.int32)[:, None]
    sending = jnp.logical_and(destination == own_holder[None, :], own_living[None, :])
    outgoing = jnp.where(sending[:, :, None, None], merged[None], jnp.zeros((), jnp.bfloat16))
    received = lax.all_to_all(outgoing, "fsdp", split_axis=0, concat_axis=0, tiled=True)
    return place_tiles(received, holder, living, row_index)


def solution(mesh):
    placed = (
        P("fsdp", "dp", None),
        P(),
        P("fsdp", "dp"),
        P(None, "dp"),
        P("dp", "fsdp"),
        P(),
        P(),
        P(),
    )
    return jax.shard_map(
        body, mesh=mesh, in_specs=placed, out_specs=P("fsdp", None, "dp"), check_vma=False
    )
```

profile of v0, /device:TPU:1, one launch (start us, length us, event | category | flops | bytes accessed | tf_op | source)
XLA Modules:
  0.0 529.9 jit_solution(8321030742287554255)
XLA Ops:
  6.5 0.7 all-gather.8.cloned.1.call-update
  7.3 0.7 all-gather.6.cloned.1.call-update
  8.1 0.8 slice_bitcast_fusion
  8.8 101.3 %all-gather.8.cloned.1.call-done = bf16[1,2176,3200]{2,1,0:T(8,128)(2,1)} async-done(((bf16[1,136,3200]{2,1,0:T(8,128)(2,1)}), bf16[1,2176,3200]{2,1,0:T(8,128)(2,1)}) %all-gather.8.cloned.1.call-update) | async-done | bytes 13926416 | tf_op jit(solution)/shard_map/all_gather | solution.py:46
  110.2 7.7 %fusion.1 = f32[2176]{0:T(1024)S(1)} fusion(bf16[1,2176,3200]{2,1,0:T(8,128)(2,1)} %all-gather.8.cloned.1.call-done), kind=kLoop, calls=%fused_computation.4 | loop fusion | flops 20887424 | bytes 13935104 | tf_op jit(solution)/shard_map/reduce_sum | solution.py:52
  117.9 47.7 %all-gather.6.cloned.1.call-done = bf16[3200,384]{1,0:T(8,128)(2,1)} async-done(((bf16[400,384]{1,0:T(8,128)(2,1)}), bf16[3200,384]{1,0:T(8,128)(2,1)}) %all-gather.6.cloned.1.call-update) | async-done | bytes 2457616 | tf_op jit(solution)/shard_map/all_gather | solution.py:56
  165.6 11.8 %fusion.5 = f32[2176,384]{1,0:T(8,128)S(1)} fusion(bf16[3200,384]{1,0:T(8,128)(2,1)} %all-gather.6.cloned.1.call-done, bf16[1,2176,3200]{2,1,0:T(8,128)(2,1)} %all-gather.8.cloned.1.call-done, f32[3200]{0:T(1024)S(1)} %copy-done.4, f32[2176]{0:T(1024)S(1)} %add_rsqrt_fusion.2), kind=kOutput, calls=%fused_computation.11 | convolution fusion | flops 5375590400 | bytes 19747840 | tf_op jit(solution)/shard_map/dot_general | solution.py:54
  177.5 0.6 multiply_reduce_fusion
  178.2 65.0 %all-reduce.1 = (f32[2176]{0:T(1024)S(1)}, f32[2176]{0:T(1024)S(1)}) all-reduce(f32[2176]{0:T(1024)S(1)} %get-tuple-element.6, f32[2176]{0:T(1024)S(1)} %get-tuple-element.5), channel_id=1, replica_groups=mesh['fsdp'=8,'dp'=16] {'dp'}, use_global_device_ids=true, to_apply=%region_3.0 | all-reduce | flops 4352 | bytes 34816 | tf_op jit(solution)/shard_map/psum | solution.py:62
  243.2 0.9 reshape.243
  244.1 1.1 fusion.15
  245.2 0.1 reshape.242
  245.3 0.1 reshape.241
  245.5 3.2 fusion.32
  248.7 4.9 fusion.12
  253.6 0.1 reshape.244
  253.7 0.8 concatenate.3
  254.6 27.5 %all_gather.19 = bf16[128,3200]{0,1:T(8,128)(2,1)} all-gather(bf16[128,400]{0,1:T(8,128)(2,1)S(1)} %copy-done.1), channel_id=1, replica_groups=mesh['fsdp'=8,'dp'=16] {'fsdp'}, dimensions={1}, use_global_device_ids=true | all-gather | bytes 921600 | tf_op jit(solution)/shard_map/all_gather | solution.py:98
  282.1 15.1 %all-to-all-start = ((bf16[128,16,200]{0,2,1:T(8,128)(2,1)}), bf16[128,16,200]{0,2,1:T(8,128)(2,1)S(1)}, u32[]{:S(2)}, u32[]{:S(2)}) async-start(bf16[128,16,200]{0,2,1:T(8,128)(2,1)} %bitcast.12), calls=%async_computation | async-start | bytes 1638400 | tf_op jit(solution)/shard_map/all_to_all | solution.py:99
  297.4 0.8 dynamic_slice.15
  298.2 2.5 constant_dynamic-slice_fusion
  300.7 0.8 copy.37
  301.5 14.2 %all-to-all-done = bf16[128,16,200]{0,2,1:T(8,128)(2,1)S(1)} async-done(((bf16[128,16,200]{0,2,1:T(8,128)(2,1)}), bf16[128,16,200]{0,2,1:T(8,128)(2,1)S(1)}, u32[]{:S(2)}, u32[]{:S(2)}) %all-to-all-start) | async-done | bytes 819232 | tf_op jit(solution)/shard_map/all_to_all | solution.py:99
  315.7 31.7 %all-gather.10.cloned.1.call-done = bf16[34816,128]{1,0:T(8,128)(2,1)} async-done(((bf16[2176,128]{1,0:T(8,128)(2,1)}), bf16[34816,128]{1,0:T(8,128)(2,1)}) %all-gather.10.cloned.1.call-update) | async-done | bytes 8912912 | tf_op jit(solution)/shard_map/all_gather | solution.py:100
  347.3 10.8 %convolution_convert_fusion.1 = bf16[16,2176,200]{1,2,0:T(8,128)(2,1)} fusion(bf16[16,2176,128]{2,1,0:T(8,128)(2,1)} %bitcast.53, bf16[128,16,200]{0,2,1:T(8,128)(2,1)S(1)} %all-to-all-done), kind=kOutput, calls=%fused_computation.8 | convolution fusion | flops 1789542400 | bytes 23658496 | tf_op jit(solution)/shard_map/hsc,hcd->hsd/dot_general | solution.py:101
  358.2 7.3 %convert_reduce_fusion = f32[2176,200]{0,1:T(8,128)S(1)} fusion(bf16[16,2176,200]{1,2,0:T(8,128)(2,1)} %convolution_convert_fusion.1), kind=kLoop, calls=%fused_computation.7 | loop fusion | flops 13491200 | bytes 15667200 | tf_op jit(solution)/shard_map/reduce_sum | solution.py:107
  365.5 0.3 fusion.13
  365.8 0.4 fusion.31
  366.1 0.2 copy.30
  366.4 1.0 reshape.245
  367.4 0.2 copy.32
  367.6 1.1 reshape.246
  368.7 4.9 copy.33
  373.5 3.9 stack_reshape.7
  377.4 4.9 copy.31
  382.3 3.8 stack_reshape.6
  386.1 1.2 pad_maximum_fusion
  387.3 3.3 broadcast_select_fusion
  390.7 5.0 all-to-all-start.1
  395.6 0.1 reshape.250
  395.8 0.1 reduce
  396.0 90.6 %all-to-all-done.1 = bf16[8,2,256,800]{2,3,1,0:T(8,128)(2,1)} async-done(((bf16[8,2,256,800]{2,3,1,0:T(8,128)(2,1)}), bf16[8,2,256,800]{2,3,1,0:T(8,128)(2,1)}, u32[]{:S(2)}, u32[]{:S(2)}) %all-to-all-start.1) | async-done | bytes 6553632 | tf_op jit(solution)/shard_map/all_to_all | solution.py:118
  486.6 11.1 %copy.34 = bf16[8,2,256,800]{3,2,1,0:T(8,128)(2,1)} copy(bf16[8,2,256,800]{2,3,1,0:T(8,128)(2,1)} %all-to-all-done.1) | data formatting | bytes 13107200 | tf_op jit(solution)/shard_map/all_to_all | solution.py:118
  497.7 14.7 %reshape.247 = bf16[16,204800]{1,0:T(8,128)(2,1)} reshape(bf16[8,2,256,800]{3,2,1,0:T(8,128)(2,1)} %copy.34) | data formatting | bytes 13107200 | tf_op jit(solution)/shard_map/reshape | solution.py:39
  512.4 4.0 convolution_convert_fusion
  516.4 1.6 reshape.258
  518.0 2.8 reshape.248
  520.8 2.3 copy.35
  (28 shorter events, 0.5 us)
Async XLA Ops:
  6.5 103.6 %all-gather.8.cloned.1.call-start = ((), (), s32[]{:S(2)}) async-start(), calls=%async_computation.3 | async-start | bytes 14796800 | tf_op jit(solution)/shard_map/all_gather | solution.py:46
  7.3 158.4 %all-gather.6.cloned.1.call-start = ((), (), s32[]{:S(2)}) async-start(), calls=%async_computation.2 | async-start | bytes 2764800 | tf_op jit(solution)/shard_map/all_gather | solution.py:56
  8.0 339.3 %all-gather.10.cloned.1.call-start = ((), (), s32[]{:S(2)}) async-start(), calls=%async_computation.4 | async-start | bytes 9469952 | tf_op jit(solution)/shard_map/all_gather | solution.py:100
  8.8 156.8 %copy-start.4 = (f32[3200]{0:T(1024)S(1)}, f32[3200]{0:T(1024)}, u32[]{:S(2)}) copy-start(f32[3200]{0:T(1024)} %param.9) | copy-start | bytes 38404
  245.3 3.4 copy-start
  248.7 5.9 %copy-start.1 = (bf16[128,400]{0,1:T(8,128)(2,1)S(1)}, bf16[128,400]{0,1:T(8,128)(2,1)}, u32[]{:S(2)}) copy-start(bf16[128,400]{0,1:T(8,128)(2,1)} %param.12) | copy-start | bytes 307204
  248.7 48.5 %copy-start.2 = (s32[8,2]{0,1:T(2,128)S(1)}, s32[8,2]{0,1:T(2,128)}, u32[]{:S(2)}) copy-start(s32[8,2]{0,1:T(2,128)} %param.15) | copy-start | bytes 196
  248.7 48.5 %copy-start.3 = (s32[8,2]{0,1:T(2,128)S(1)}, s32[8,2]{0,1:T(2,128)}, u32[]{:S(2)}) copy-start(s32[8,2]{0,1:T(2,128)} %param.14) | copy-start | bytes 196
  282.1 33.6 %all-to-all-start = ((bf16[128,16,200]{0,2,1:T(8,128)(2,1)}), bf16[128,16,200]{0,2,1:T(8,128)(2,1)S(1)}, u32[]{:S(2)}, u32[]{:S(2)}) async-start(bf16[128,16,200]{0,2,1:T(8,128)(2,1)} %bitcast.12), calls=%async_computation | async-start | bytes 1638400 | tf_op jit(solution)/shard_map/all_to_all | solution.py:99
  390.7 95.9 %all-to-all-start.1 = ((bf16[8,2,256,800]{2,3,1,0:T(8,128)(2,1)}), bf16[8,2,256,800]{2,3,1,0:T(8,128)(2,1)}, u32[]{:S(2)}, u32[]{:S(2)}) async-start(bf16[8,2,256,800]{2,3,1,0:T(8,128)(2,1)} %broadcast_select_fusion), calls=%async_computation.1 | async-start | bytes 13107200 | tf_op jit(solution)/shard_map/all_to_all | solution.py:118
Sparse Core Ops, SparseCore 0:
  9.8 100.3 all-gather.7
  111.8 53.8 all-gather.5
  254.7 92.5 all-gather.9
where the time goes:
time: 535 us; the launch traced here: 530 us
  waiting for transfers between devices  287 us (54%)
  blocking collectives  92.5 us (17%)
  local copies, waits for them, and re-layouts  59.9 us (11%)
  matrix products  34.7 us (6%)
  other arithmetic  22 us (4%)
  starting transfers between devices  20.1 us (4%)
  between operations  13.6 us (3%)
    all_gather x1, waiting for transfers between devices, body(): gathered = lax.all_gather(own_rows, 'dp', axis=0, tiled=True)  101 us
    all_to_all x1, waiting for transfers between devices, body(): lax.all_to_all(outgoing, 'fsdp', split_axis=0, concat_axis=0, tiled=True)  90.6 us
    psum x1, blocking collectives, body(): lax.psum((jnp.sum(queries * queries, axis=-1), jnp.sum(keys_part * keys_p...  65 us
    all_gather x1, waiting for transfers between devices, body(): lax.all_gather(qkv_weight, 'fsdp', axis=0, tiled=True)  47.7 us
    all_gather x1, waiting for transfers between devices, body(): all_heads = lax.all_gather(head_out, 'dp', axis=0, tiled=False)  31.7 us
    all_gather x1, blocking collectives, body(): head_rows = lax.all_gather(out_weight, 'fsdp', axis=1, tiled=True)  27.5 us
    all_to_all x1, starting transfers between devices, body(): lax.all_to_all(head_rows, 'dp', split_axis=1, concat_axis=0, tiled=True)  15.1 us
    reshape x1, local copies, waits for them, and re-layouts, place_tiles(): flattened = received.reshape(received.shape[0] * received.shape[1], -1)  14.7 us
  transfers between devices with their start and end apart: 5, of which 5 were waited for; matrix products, arithmetic and copies ran while one was open for 2% of the time, Pallas kernels for 0%

commit v1 on v0

--- a/solution.py
+++ b/solution.py
@@ -51,10 +51,17 @@
     normed = (
         values * lax.rsqrt(jnp.mean(values * values, axis=-1, keepdims=True) + EPSILON) * norm_gain
     ).astype(jnp.bfloat16)
+    change_the_outputs = lambda arr, across: jnp.concatenate(
+        jax.lax.all_to_all(
+            jnp.stack(jax.lax.axis_size(across) * [arr]),
+            axis_name=across,
+            split_axis=0,
+            concat_axis=0,
+        ),
+        axis=0,
+    )
     projected = jnp.dot(
-        normed,
-        lax.all_gather(qkv_weight, "fsdp", axis=0, tiled=True),
-        preferred_element_type=jnp.float32,
+        normed, change_the_outputs(qkv_weight, "fsdp"), preferred_element_type=jnp.float32
     )
     queries = projected[:, :HEAD_DIM]
     keys_part = projected[:, HEAD_DIM : 2 * HEAD_DIM]

time: 535 us -> 503 us (0.940)
  waiting for transfers between devices: 287 us -> 251 us
    all_gather x1 -> x0, waiting for transfers between devices: 47.7 us -> none  [body(): lax.all_gather(qkv_weight, 'fsdp', axis=0, tiled=True)]
    all_gather x1, waiting for transfers between devices: 101 us -> 114 us  [body(): gathered = lax.all_gather(own_rows, 'dp', axis=0, tiled=True)]
    all_to_all x0 -> x1, starting transfers between devices: none -> 6.19 us  [body(): jax.lax.all_to_all(jnp.stack(jax.lax.axis_size(across) * [arr]), axis_nam...]
  transfers between devices with their start and end apart: 5 -> 5, of which waited for: 5 -> 4; matrix products, arithmetic and copies ran while one was open for 2% -> 3% of each run, Pallas kernels for 0% -> 0%
where the time goes in v1:
time: 503 us; the launch traced here: 497 us
  waiting for transfers between devices  251 us (50%)
  blocking collectives  90.1 us (18%)
  local copies, waits for them, and re-layouts  61.8 us (12%)
  matrix products  33.9 us (7%)
  starting transfers between devices  24.8 us (5%)
  other arithmetic  22 us (4%)
  between operations  13.9 us (3%)
    all_gather x1, waiting for transfers between devices, body(): gathered = lax.all_gather(own_rows, 'dp', axis=0, tiled=True)  114 us
    all_to_all x1, waiting for transfers between devices, body(): lax.all_to_all(outgoing, 'fsdp', split_axis=0, concat_axis=0, tiled=True)  90.6 us
    psum x1, blocking collectives, body(): lax.psum((jnp.sum(queries * queries, axis=-1), jnp.sum(keys_part * keys_p...  60.2 us
    all_gather x1, waiting for transfers between devices, body(): all_heads = lax.all_gather(head_out, 'dp', axis=0, tiled=False)  31.6 us
    all_gather x1, blocking collectives, body(): head_rows = lax.all_gather(out_weight, 'fsdp', axis=1, tiled=True)  29.9 us
    reshape x1, local copies, waits for them, and re-layouts, place_tiles(): flattened = received.reshape(received.shape[0] * received.shape[1], -1)  14.7 us
    all_to_all x1, waiting for transfers between devices, body(): lax.all_to_all(head_rows, 'dp', split_axis=1, concat_axis=0, tiled=True)  14.2 us
    all_to_all x1, starting transfers between devices, body(): lax.all_to_all(head_rows, 'dp', split_axis=1, concat_axis=0, tiled=True)  13.6 us
  transfers between devices with their start and end apart: 5, of which 4 were waited for; matrix products, arithmetic and copies ran while one was open for 3% of the time, Pallas kernels for 0%

profile of v1, /device:TPU:1, one launch (start us, length us, event | category | flops | bytes accessed | tf_op | source)
XLA Modules:
  0.0 497.1 jit_solution(13555578694489103789)
XLA Ops:
  6.5 0.7 all-gather.5.cloned.1.call-update
  7.3 2.6 stack.4
  9.9 6.2 %all-to-all-start = ((bf16[8,400,384]{2,1,0:T(8,128)(2,1)}), bf16[8,400,384]{2,1,0:T(8,128)(2,1)S(1)}, u32[]{:S(2)}, u32[]{:S(2)}) async-start(bf16[8,400,384]{2,1,0:T(8,128)(2,1)} %stack.4), calls=%async_computation | async-start | bytes 4915200 | tf_op jit(solution)/shard_map/all_to_all | solution.py:55
  16.1 113.5 %all-gather.5.cloned.1.call-done = bf16[1,2176,3200]{2,1,0:T(8,128)(2,1)} async-done(((bf16[1,136,3200]{2,1,0:T(8,128)(2,1)}), bf16[1,2176,3200]{2,1,0:T(8,128)(2,1)}) %all-gather.5.cloned.1.call-update) | async-done | bytes 13926416 | tf_op jit(solution)/shard_map/all_gather | solution.py:46
  129.7 7.7 %fusion.1 = f32[2176]{0:T(1024)S(1)} fusion(bf16[1,2176,3200]{2,1,0:T(8,128)(2,1)} %all-gather.5.cloned.1.call-done), kind=kLoop, calls=%fused_computation.4 | loop fusion | flops 20887424 | bytes 13935104 | tf_op jit(solution)/shard_map/reduce_sum | solution.py:52
  137.4 11.0 %fusion.5 = f32[2176,384]{1,0:T(8,128)S(1)} fusion(bf16[3200,384]{1,0:T(8,128)(2,1)S(1)} %bitcast.55, bf16[1,2176,3200]{2,1,0:T(8,128)(2,1)} %all-gather.5.cloned.1.call-done, f32[3200]{0:T(1024)S(1)} %copy-done.5, f32[2176]{0:T(1024)S(1)} %add_rsqrt_fusion.2), kind=kOutput, calls=%fused_computation.11 | convolution fusion | flops 5375590400 | bytes 19747840 | tf_op jit(solution)/shard_map/dot_general | solution.py:63
  148.5 0.6 multiply_reduce_fusion
  149.2 60.2 %all-reduce.1 = (f32[2176]{0:T(1024)S(1)}, f32[2176]{0:T(1024)S(1)}) all-reduce(f32[2176]{0:T(1024)S(1)} %get-tuple-element.6, f32[2176]{0:T(1024)S(1)} %get-tuple-element.5), channel_id=1, replica_groups=mesh['fsdp'=8,'dp'=16] {'dp'}, use_global_device_ids=true, to_apply=%region_3.0 | all-reduce | flops 4352 | bytes 34816 | tf_op jit(solution)/shard_map/psum | solution.py:69
  209.4 0.9 reshape.249
  210.3 1.1 fusion.15
  211.4 0.1 reshape.248
  211.5 0.1 reshape.247
  211.7 3.2 fusion.32
  214.9 4.9 fusion.12
  219.8 0.1 reshape.250
  219.9 0.8 concatenate.3
  220.8 29.9 %all_gather.15 = bf16[128,3200]{0,1:T(8,128)(2,1)} all-gather(bf16[128,400]{0,1:T(8,128)(2,1)S(1)} %copy-done.1), channel_id=1, replica_groups=mesh['fsdp'=8,'dp'=16] {'fsdp'}, dimensions={1}, use_global_device_ids=true | all-gather | bytes 921600 | tf_op jit(solution)/shard_map/all_gather | solution.py:105
  250.7 13.6 %all-to-all-start.1 = ((bf16[128,16,200]{0,2,1:T(8,128)(2,1)}), bf16[128,16,200]{0,2,1:T(8,128)(2,1)S(1)}, u32[]{:S(2)}, u32[]{:S(2)}) async-start(bf16[128,16,200]{0,2,1:T(8,128)(2,1)} %bitcast.13), calls=%async_computation.1 | async-start | bytes 1638400 | tf_op jit(solution)/shard_map/all_to_all | solution.py:106
  264.4 0.1 and_convert_fusion
  264.4 0.8 dynamic_slice.15
  265.2 2.5 constant_dynamic-slice_fusion
  267.7 0.8 copy.37
  268.5 14.2 %all-to-all-done.1 = bf16[128,16,200]{0,2,1:T(8,128)(2,1)S(1)} async-done(((bf16[128,16,200]{0,2,1:T(8,128)(2,1)}), bf16[128,16,200]{0,2,1:T(8,128)(2,1)S(1)}, u32[]{:S(2)}, u32[]{:S(2)}) %all-to-all-start.1) | async-done | bytes 819232 | tf_op jit(solution)/shard_map/all_to_all | solution.py:106
  282.7 31.6 %all-gather.7.cloned.1.call-done = bf16[34816,128]{1,0:T(8,128)(2,1)} async-done(((bf16[2176,128]{1,0:T(8,128)(2,1)}), bf16[34816,128]{1,0:T(8,128)(2,1)}) %all-gather.7.cloned.1.call-update) | async-done | bytes 8912912 | tf_op jit(solution)/shard_map/all_gather | solution.py:107
  314.3 10.8 %convolution_convert_fusion.1 = bf16[16,2176,200]{1,2,0:T(8,128)(2,1)} fusion(bf16[16,2176,128]{2,1,0:T(8,128)(2,1)} %bitcast.54, bf16[128,16,200]{0,2,1:T(8,128)(2,1)S(1)} %all-to-all-done.1), kind=kOutput, calls=%fused_computation.8 | convolution fusion | flops 1789542400 | bytes 23658496 | tf_op jit(solution)/shard_map/hsc,hcd->hsd/dot_general | solution.py:108
  325.1 7.3 %convert_reduce_fusion = f32[2176,200]{0,1:T(8,128)S(1)} fusion(bf16[16,2176,200]{1,2,0:T(8,128)(2,1)} %convolution_convert_fusion.1), kind=kLoop, calls=%fused_computation.7 | loop fusion | flops 13491200 | bytes 15667200 | tf_op jit(solution)/shard_map/reduce_sum | solution.py:114
  332.5 0.3 fusion.13
  332.7 0.4 fusion.31
  333.1 0.2 copy.30
  333.3 1.0 reshape.251
  334.4 0.2 copy.32
  334.6 1.1 reshape.252
  335.6 4.9 copy.33
  340.5 3.9 stack_reshape.7
  344.4 4.9 copy.31
  349.2 3.8 stack_reshape.6
  353.1 1.2 pad_maximum_fusion
  354.3 3.3 broadcast_select_fusion
  357.6 5.0 %all-to-all-start.2 = ((bf16[8,2,256,800]{2,3,1,0:T(8,128)(2,1)}), bf16[8,2,256,800]{2,3,1,0:T(8,128)(2,1)}, u32[]{:S(2)}, u32[]{:S(2)}) async-start(bf16[8,2,256,800]{2,3,1,0:T(8,128)(2,1)} %broadcast_select_fusion), calls=%async_computation.2 | async-start | bytes 13107200 | tf_op jit(solution)/shard_map/all_to_all | solution.py:125
  362.6 0.1 reshape.256
  362.8 0.1 reduce
  362.9 90.6 %all-to-all-done.2 = bf16[8,2,256,800]{2,3,1,0:T(8,128)(2,1)} async-done(((bf16[8,2,256,800]{2,3,1,0:T(8,128)(2,1)}), bf16[8,2,256,800]{2,3,1,0:T(8,128)(2,1)}, u32[]{:S(2)}, u32[]{:S(2)}) %all-to-all-start.2) | async-done | bytes 6553632 | tf_op jit(solution)/shard_map/all_to_all | solution.py:125
  453.6 11.1 %copy.34 = bf16[8,2,256,800]{3,2,1,0:T(8,128)(2,1)} copy(bf16[8,2,256,800]{2,3,1,0:T(8,128)(2,1)} %all-to-all-done.2) | data formatting | bytes 13107200 | tf_op jit(solution)/shard_map/all_to_all | solution.py:125
  464.6 14.7 %reshape.253 = bf16[16,204800]{1,0:T(8,128)(2,1)} reshape(bf16[8,2,256,800]{3,2,1,0:T(8,128)(2,1)} %copy.34) | data formatting | bytes 13107200 | tf_op jit(solution)/shard_map/reshape | solution.py:39
  479.4 4.0 convolution_convert_fusion
  483.3 1.6 reshape.264
  485.0 2.8 reshape.254
  487.7 2.3 copy.35
  (30 shorter events, 0.4 us)
Async XLA Ops:
  6.5 9.6 %copy-start.2 = (f32[2,128]{1,0:T(2,128)S(1)}, f32[2,128]{1,0:T(2,128)}, u32[]{:S(2)}) copy-start(f32[2,128]{1,0:T(2,128)} %param.11) | copy-start | bytes 3076
  6.5 123.1 %all-gather.5.cloned.1.call-start = ((), (), s32[]{:S(2)}) async-start(), calls=%async_computation.3 | async-start | bytes 14796800 | tf_op jit(solution)/shard_map/all_gather | solution.py:46
  9.9 127.5 %all-to-all-start = ((bf16[8,400,384]{2,1,0:T(8,128)(2,1)}), bf16[8,400,384]{2,1,0:T(8,128)(2,1)S(1)}, u32[]{:S(2)}, u32[]{:S(2)}) async-start(bf16[8,400,384]{2,1,0:T(8,128)(2,1)} %stack.4), calls=%async_computation | async-start | bytes 4915200 | tf_op jit(solution)/shard_map/all_to_all | solution.py:55
  16.0 298.3 %all-gather.7.cloned.1.call-start = ((), (), s32[]{:S(2)}) async-start(), calls=%async_computation.4 | async-start | bytes 9469952 | tf_op jit(solution)/shard_map/all_gather | solution.py:107
  16.1 121.3 %copy-start.5 = (f32[3200]{0:T(1024)S(1)}, f32[3200]{0:T(1024)}, u32[]{:S(2)}) copy-start(f32[3200]{0:T(1024)} %param.9) | copy-start | bytes 38404
  211.5 3.4 copy-start
  214.9 5.9 %copy-start.1 = (bf16[128,400]{0,1:T(8,128)(2,1)S(1)}, bf16[128,400]{0,1:T(8,128)(2,1)}, u32[]{:S(2)}) copy-start(bf16[128,400]{0,1:T(8,128)(2,1)} %param.12) | copy-start | bytes 307204
  214.9 49.3 %copy-start.3 = (s32[8,2]{0,1:T(2,128)S(1)}, s32[8,2]{0,1:T(2,128)}, u32[]{:S(2)}) copy-start(s32[8,2]{0,1:T(2,128)} %param.15) | copy-start | bytes 196
  214.9 49.3 %copy-start.4 = (s32[8,2]{0,1:T(2,128)S(1)}, s32[8,2]{0,1:T(2,128)}, u32[]{:S(2)}) copy-start(s32[8,2]{0,1:T(2,128)} %param.14) | copy-start | bytes 196
  250.7 32.1 %all-to-all-start.1 = ((bf16[128,16,200]{0,2,1:T(8,128)(2,1)}), bf16[128,16,200]{0,2,1:T(8,128)(2,1)S(1)}, u32[]{:S(2)}, u32[]{:S(2)}) async-start(bf16[128,16,200]{0,2,1:T(8,128)(2,1)} %bitcast.13), calls=%async_computation.1 | async-start | bytes 1638400 | tf_op jit(solution)/shard_map/all_to_all | solution.py:106
  357.6 95.9 %all-to-all-start.2 = ((bf16[8,2,256,800]{2,3,1,0:T(8,128)(2,1)}), bf16[8,2,256,800]{2,3,1,0:T(8,128)(2,1)}, u32[]{:S(2)}, u32[]{:S(2)}) async-start(bf16[8,2,256,800]{2,3,1,0:T(8,128)(2,1)} %broadcast_select_fusion), calls=%async_computation.2 | async-start | bytes 13107200 | tf_op jit(solution)/shard_map/all_to_all | solution.py:125
Sparse Core Ops, SparseCore 0:
  9.8 119.8 all-gather.4
  220.9 93.3 all-gather.6
